TPU v7x, 32 devices: a whole 2x2x4 slice. The times are simulated.
32 devices in a mesh: groups: 2 (over x), wide: 16 (over z, y, core).
Axes of the slice: x: 2, y: 2, z: 4, core: 2. Of those that a mesh axis runs over, the one named last changes fastest.
Arguments:
- query_act: bfloat16 [4096, 2048], P(('groups', 'wide')), parts along dimension 0, may hold values from -6 to 6
- query_grad: bfloat16 [4096, 4096], P(('groups', 'wide')), parts along dimension 0, may hold values from -6 to 6
- query_positions: int32 [4096], P(('groups', 'wide')), parts along dimension 0, may hold values from 0 to 4095
- act_basis: bfloat16 [2048, 1024], P(None, 'wide'), may hold values from -0.125 to 0.125
- grad_basis: bfloat16 [4096, 2048], P(None, 'wide'), may hold values from -0.09375 to 0.09375
- eig_values: bfloat16 [1024, 2048], P('wide'), may hold values from 0.05 to 50, as said below
- damping_index: int32 [12], P('groups'), parts along dimension 0, may hold values from 0 to 8
- train_act_rot: bfloat16 [1024, 6144], P(None, 'wide'), may hold values from -6 to 6
- train_grad_rot: bfloat16 [2048, 6144], P(None, 'wide'), may hold values from -6 to 6
- train_positions: int32 [6144], P('wide'), may hold values from 0 to 4095
Outputs:
- influences: float32 [12, 6144], P('groups', 'wide'), parts along dimension 0
There are 2 independent parts, one for each index of `groups`. A program takes and returns all parts, laid end to end along the dimension named above; an argument that names none is the same for every part. Nothing has to cross between parts.
Inputs may be any that keep to these rules, and one draw needn't show every extreme that they name: `eig_values`: positive corrected eigenvalues.
All inputs are finite; a program needn't handle non-finite values.
Results may differ from a plain program's by a relative error of at most 0.0059.
Values may be sent and summed in bfloat16 or wider, within the bound.
No kernel may reach another device: no remote copies, remote signals or barrier semaphores. Data moves between devices by JAX's collectives and lax.ppermute only.
A program may use at most 128 MiB of HBM per device.

v0:
```python
import math
import jax
import jax.numpy as jnp
from jax import lax
from jax.sharding import PartitionSpec as P

EIG_IN = 1024
EIG_OUT = 2048
PROMPT = 1024


def score_rows(grad_rows, eig_rows, dampings, train_act_rot, train_grad_rot):
    acts_rows = train_act_rot.astype(jnp.float32)
    grad_wide = grad_rows.astype(jnp.float32)
    eig_wide = eig_rows.astype(jnp.float32)
    results = []
    for damping in range(dampings.shape[0]):
        precond = (grad_wide / (eig_wide + dampings[damping])).astype(jnp.bfloat16)
        projected = jnp.dot(precond, train_grad_rot, preferred_element_type=jnp.float32)
        results.append(jnp.sum(projected * acts_rows, axis=0))
    return jnp.stack(results)


def shards(
    query_act,
    query_grad,
    query_positions,
    act_basis,
    grad_basis,
    eig_values,
    damping_index,
    train_act_rot,
    train_grad_rot,
    train_positions,
):
    act_full = jnp.dot(
        query_act,
        lax.all_gather(act_basis, "wide", axis=1, tiled=True),
        preferred_element_type=jnp.float32,
    )
    grad_full = jnp.dot(
        query_grad,
        lax.all_gather(grad_basis, "wide", axis=1, tiled=True),
        preferred_element_type=jnp.float32,
    )
    act_rot = act_full.astype(jnp.bfloat16)
    grad_rot = grad_full.astype(jnp.bfloat16)
    query_weight = jnp.where(query_positions >= PROMPT, 1.0, 0.0).astype(jnp.bfloat16)
    grad_kept = grad_rot * query_weight[:, None]
    eig_total = lax.psum(jnp.sum(eig_values.astype(jnp.float32)), "wide")
    mean_eig = eig_total / (EIG_IN * EIG_OUT)
    dampings = mean_eig * jnp.exp2(damping_index.astype(jnp.float32) - 4.0)
    partial_whole = lax.dot_general(
        act_rot, grad_kept, (((0,), (0,)), ((), ())), preferred_element_type=jnp.float32
    )
    query_gradient = lax.psum(partial_whole, "wide").astype(jnp.bfloat16)
    totals = score_rows(
        query_gradient,
        lax.all_gather(eig_values, "wide", axis=0, tiled=True),
        dampings,
        train_act_rot,
        train_grad_rot,
    )
    query_count = query_act.shape[0] * lax.axis_size("wide")
    factor = mean_eig * (1.0 / math.sqrt(float(query_count) * EIG_IN * EIG_OUT))
    train_weight = jnp.where(train_positions >= PROMPT, 1.0, 0.0).astype(jnp.float32)
    return totals * factor * train_weight[None, :]


def solution(mesh):
    in_specs = (
        P(("groups", "wide"), None),
        P(("groups", "wide"), None),
        P(("groups", "wide")),
        P(None, "wide"),
        P(None, "wide"),
        P("wide", None),
        P("groups"),
        P(None, "wide"),
        P(None, "wide"),
        P("wide"),
    )
    out_specs = P("groups", "wide")
    return jax.shard_map(shards, mesh=mesh, in_specs=in_specs, out_specs=out_specs, check_vma=False)
```

profile of v0, /device:TPU:1, one launch (start us, length us, event | category | flops | bytes accessed | tf_op | source)
XLA Modules:
  0.0 428.8 jit_solution(4725387925321449047)
XLA Ops:
  6.5 0.0 copy-start
  6.5 0.0 all-gather.6.cloned.1.call-start
  6.5 0.7 all-gather.6.cloned.1.call-update
  7.3 0.0 all-gather.4.cloned.1.call-start
  7.3 0.7 all-gather.4.cloned.1.call-update
  8.0 0.0 all-gather.8.cloned.1.call-start
  8.1 0.7 all-gather.8.cloned.1.call-update
  8.7 1.7 convert_reduce_fusion
  10.4 0.7 fusion.38
  11.1 0.7 compare_select_fusion
  11.8 0.0 copy-start.1
  11.8 130.6 %all-gather.6.cloned.1.call-done = bf16[4096,2048]{1,0:T(8,128)(2,1)} async-done(((bf16[4096,128]{1,0:T(8,128)(2,1)}), bf16[4096,2048]{1,0:T(8,128)(2,1)}) %all-gather.6.cloned.1.call-update) | async-done | bytes 16777232 | tf_op jit(solution)/shard_map/all_gather | solution.py:43
  142.4 8.4 %fusion.18 = bf16[128,2048]{1,0:T(8,128)(2,1)S(1)} fusion(bf16[128,4096]{1,0:T(8,128)(2,1)} %param.11, bf16[4096,2048]{1,0:T(8,128)(2,1)} %all-gather.6.cloned.1.call-done, bf16[128]{0:T(256)(128)(2,1)S(1)} %fusion.38), kind=kOutput, calls=%fused_computation.31 | convolution fusion | flops 2148007936 | bytes 18350336 | tf_op jit(solution)/shard_map/dot_general | solution.py:41
  150.8 42.5 %all-gather.4.cloned.1.call-done = bf16[2048,1024]{0,1:T(8,128)(2,1)} async-done(((bf16[2048,64]{0,1:T(8,128)(2,1)}), bf16[2048,1024]{0,1:T(8,128)(2,1)}) %all-gather.4.cloned.1.call-update) | async-done | bytes 4194320 | tf_op jit(solution)/shard_map/all_gather | solution.py:38
  193.3 0.0 copy-done.1
  193.3 8.1 %fusion.37 = f32[1024,2048]{1,0:T(8,128)} fusion(bf16[128,2048]{1,0:T(8,128)(2,1)S(1)} %fusion.18, bf16[128,2048]{1,0:T(8,128)(2,1)S(1)} %copy-done.1, bf16[2048,1024]{0,1:T(8,128)(2,1)} %all-gather.4.cloned.1.call-done), kind=kOutput, calls=%fused_computation.39 | convolution fusion | flops 1073872896 | bytes 13631488 | tf_op jit(solution)/shard_map/dot_general | solution.py:53
  201.4 0.0 copy-start.5
  201.4 0.0 copy-start.4
  201.4 195.6 %all-reduce.2 = (bf16[1024,2048]{1,0:T(8,128)(2,1)}, f32[]{:T(128)}) all-reduce(f32[1024,2048]{1,0:T(8,128)} %fusion.37, f32[]{:T(128)} %convert_reduce_fusion), channel_id=1, replica_groups=mesh['groups'=2,'wide'=16] {'wide'}, use_global_device_ids=true, to_apply=%region_0.1 | all-reduce | flops 2097153 | bytes 12582920 | tf_op jit(solution)/shard_map/psum | solution.py:56
  397.7 0.0 copy-done.5
  397.8 0.7 fusion.39
  398.4 0.0 all-gather.8.cloned.1.call-done
  398.4 0.0 copy-done
  398.4 0.0 copy-done.4
  398.4 0.0 copy-start.2
  398.4 0.0 copy-start.3
  398.5 7.0 %fusion.24 = f32[384]{0:T(512)S(1)} fusion(bf16[1024,384]{1,0:T(8,128)(2,1)S(1)} %copy-done.4, bf16[2048,384]{1,0:T(8,128)(2,1)S(1)} %copy-done, bf16[1024,2048]{1,0:T(8,128)(2,1)} %get-tuple-element.5, bf16[1024,2048]{1,0:T(8,128)(2,1)} %all-gather.8.cloned.1.call-done, f32[]{:T(128)} %bitcast.5), kind=kOutput, calls=%fused_computation.37 | convolution fusion | flops 1622277760 | bytes 10749444 | tf_op jit(solution)/shard_map/dot_general | solution.py:19
  405.5 0.0 copy-done.2
  405.5 0.0 copy-done.3
  405.5 3.0 fusion.23
  408.5 3.1 fusion.22
  411.6 3.0 fusion.21
  414.6 3.3 fusion.20
  417.9 3.0 fusion.19
  421.6 0.6 multiply_multiply_fusion
  (8 shorter events, 0.1 us)
Async XLA Ops:
  6.5 391.9 %copy-start = (bf16[2048,384]{1,0:T(8,128)(2,1)S(1)}, bf16[2048,384]{1,0:T(8,128)(2,1)}, u32[]{:S(2)}) copy-start(bf16[2048,384]{1,0:T(8,128)(2,1)} %param.18) | copy-start | bytes 4718596
  6.5 135.9 %all-gather.6.cloned.1.call-start = ((), (), s32[]{:S(2)}) async-start(), calls=%async_computation.1 | async-start | bytes 17825792 | tf_op jit(solution)/shard_map/all_gather | solution.py:43
  7.3 186.1 %all-gather.4.cloned.1.call-start = ((), (), s32[]{:S(2)}) async-start(), calls=%async_computation | async-start | bytes 4456448 | tf_op jit(solution)/shard_map/all_gather | solution.py:38
  8.0 390.4 %all-gather.8.cloned.1.call-start = ((), (), s32[]{:S(2)}) async-start(), calls=%async_computation.2 | async-start | bytes 4456448 | tf_op jit(solution)/shard_map/all_gather | solution.py:59
  11.8 181.6 %copy-start.1 = (bf16[128,2048]{1,0:T(8,128)(2,1)S(1)}, bf16[128,2048]{1,0:T(8,128)(2,1)}, u32[]{:S(2)}) copy-start(bf16[128,2048]{1,0:T(8,128)(2,1)} %param.10) | copy-start | bytes 1572868
  201.4 196.3 %copy-start.5 = (s32[6]{0:T(128)S(1)}, s32[6]{0:T(128)}, u32[]{:S(2)}) copy-start(s32[6]{0:T(128)} %param.16) | copy-start | bytes 76
  201.4 197.0 %copy-start.4 = (bf16[1024,384]{1,0:T(8,128)(2,1)S(1)}, bf16[1024,384]{1,0:T(8,128)(2,1)}, u32[]{:S(2)}) copy-start(bf16[1024,384]{1,0:T(8,128)(2,1)} %param.17) | copy-start | bytes 2359300
  398.4 7.0 %copy-start.2 = (bf16[1024,2048]{1,0:T(8,128)(2,1)S(1)}, bf16[1024,2048]{1,0:T(8,128)(2,1)}, u32[]{:S(2)}) copy-start(bf16[1024,2048]{1,0:T(8,128)(2,1)} %all-gather.8.cloned.1.call-done) | copy-start | bytes 12582916
  398.4 7.0 %copy-start.3 = (bf16[1024,2048]{1,0:T(8,128)(2,1)S(1)}, bf16[1024,2048]{1,0:T(8,128)(2,1)}, u32[]{:S(2)}) copy-start(bf16[1024,2048]{1,0:T(8,128)(2,1)} %get-tuple-element.5) | copy-start | bytes 12582916
Sparse Core Ops, SparseCore 0:
  9.5 132.8 all-gather.5
  144.6 48.7 all-gather.3
  195.5 67.8 all-gather.7
where the time goes:
time: 429 us
  blocking collectives  196 us (46%)
  waiting for transfers between devices  175 us (41%)
  matrix products  39 us (9%)
  between operations  14.5 us (3%)
    psum x1, blocking collectives, shards(): query_gradient = lax.psum(partial_whole, 'wide').astype(jnp.bfloat16)  196 us
    all_gather x1, waiting for transfers between devices, shards(): lax.all_gather(grad_basis, 'wide', axis=1, tiled=True)  131 us
    all_gather x1, waiting for transfers between devices, shards(): lax.all_gather(act_basis, 'wide', axis=1, tiled=True)  42.5 us
    dot_general x6, matrix products, score_rows(): jnp.dot(precond, train_grad_rot, preferred_element_type=jnp.float32)  22.4 us
  transfers between devices with their start and end apart: 3, of which 2 were waited for; matrix products, arithmetic and copies ran while one was open for 5% of the time, Pallas kernels for 0%

commit v1 on v0

--- a/solution.py
+++ b/solution.py
@@ -7,6 +7,14 @@
 EIG_IN = 1024
 EIG_OUT = 2048
 PROMPT = 1024
+
+
+def plan_tiles(w_in, dim_no):
+    w_in = jnp.moveaxis(w_in, 0, dim_no)
+    next_value = w_in.shape
+    return w_in.reshape(
+        *next_value[:dim_no], next_value[dim_no] * next_value[dim_no + 1], *next_value[dim_no + 2 :]
+    )
 
 
 def score_rows(grad_rows, eig_rows, dampings, train_act_rot, train_grad_rot):
@@ -33,10 +41,19 @@
     train_grad_rot,
     train_positions,
 ):
+
+    def put_the_sums_all(xx, axis_tag, dim_at):
+        num = lax.axis_size(axis_tag)
+        store = [(ii, (ii + 1) % num) for ii in range(num)]
+        line_up = [xx]
+        while len(line_up) < num:
+            line_up.append(lax.ppermute(line_up[-1], axis_tag, store))
+        plain = lax.axis_index(axis_tag)
+        line_up = jnp.stack(line_up)[(plain - jnp.arange(num)) % num]
+        return plan_tiles(line_up, dim_at)
+
     act_full = jnp.dot(
-        query_act,
-        lax.all_gather(act_basis, "wide", axis=1, tiled=True),
-        preferred_element_type=jnp.float32,
+        query_act, put_the_sums_all(act_basis, "wide", 1), preferred_element_type=jnp.float32
     )
     grad_full = jnp.dot(
         query_grad,

time: 429 us -> 430 us (level)
  waiting for transfers between devices: 175 us -> 148 us
  local copies, waits for them, and re-layouts: 0.75 us -> 18.3 us
  starting transfers between devices: 0.08 us -> 8.93 us
    ppermute x0 -> x15, waiting for transfers between devices: none -> 148 us  [put_the_sums_all(): line_up.append(lax.ppermute(line_up[-1], axis_tag, store))]
    all_gather x1, waiting for transfers between devices: 131 us -> 0.01 us  [shards(): lax.all_gather(grad_basis, 'wide', axis=1, tiled=True)]
    all_gather x1 -> x0, waiting for transfers between devices: 42.5 us -> none  [shards(): lax.all_gather(act_basis, 'wide', axis=1, tiled=True)]
    unnamed x12 -> x27, local copies, waits for them, and re-layouts: 0.02 us -> 11.8 us
    ppermute x0 -> x15, starting transfers between devices: none -> 8.89 us  [put_the_sums_all(): line_up.append(lax.ppermute(line_up[-1], axis_tag, store))]
    gather x0 -> x1, local copies, waits for them, and re-layouts: none -> 5.07 us  [put_the_sums_all(): line_up = jnp.stack(line_up)[(plain - jnp.arange(num)) % num]]
  transfers between devices with their start and end apart: 3 -> 17, of which waited for: 2 -> 14; matrix products, arithmetic and copies ran while one was open for 5% -> 9% of each run, Pallas kernels for 0% -> 0%
where the time goes in v1:
time: 430 us; the launch traced here: 429 us
  blocking collectives  195 us (45%)
  waiting for transfers between devices  148 us (34%)
  matrix products  40 us (9%)
  local copies, waits for them, and re-layouts  18.3 us (4%)
  between operations  14.9 us (3%)
  starting transfers between devices  8.93 us (2%)
    psum x1, blocking collectives, shards(): query_gradient = lax.psum(partial_whole, 'wide').astype(jnp.bfloat16)  195 us
    ppermute x15, waiting for transfers between devices, put_the_sums_all(): line_up.append(lax.ppermute(line_up[-1], axis_tag, store))  148 us
    dot_general x6, matrix products, score_rows(): jnp.dot(precond, train_grad_rot, preferred_element_type=jnp.float32)  21.9 us
    unnamed x27, local copies, waits for them, and re-layouts  11.8 us
    dot_general x1, matrix products, shards(): lax.dot_general(act_rot, grad_kept, (((0,), (0,)), ((), ())), preferred_e...  9.87 us
    ppermute x15, starting transfers between devices, put_the_sums_all(): line_up.append(lax.ppermute(line_up[-1], axis_tag, store))  8.89 us
  transfers between devices with their start and end apart: 17, of which 14 were waited for; matrix products, arithmetic and copies ran while one was open for 9% of the time, Pallas kernels for 0%

profile of v1, /device:TPU:1, one launch (start us, length us, event | category | flops | bytes accessed | tf_op | source)
XLA Modules:
  0.0 428.8 jit_solution(15096294378719245484)
XLA Ops:
  6.5 0.7 all-gather.3.cloned.1.call-update
  7.3 2.7 collective-permute-start
  10.0 1.7 bitcast_dynamic-update-slice_fusion.15
  11.7 1.7 convert_reduce_fusion
  13.4 0.7 fusion.38
  14.1 0.7 compare_select_fusion.3
  14.8 1.2 collective-permute-start.1
  16.0 0.7 bitcast_dynamic-update-slice_fusion.14
  16.7 2.6 collective-permute-done.1
  19.3 2.5 collective-permute-start.2
  21.8 0.7 bitcast_dynamic-update-slice_fusion.13
  22.5 8.1 %collective-permute-done.2 = bf16[2048,64]{0,1:T(8,128)(2,1)S(1)} collective-permute-done((bf16[2048,64]{0,1:T(8,128)(2,1)S(1)}, bf16[2048,64]{0,1:T(8,128)(2,1)S(1)}, u32[]{:S(2)}, u32[]{:S(2)}) %collective-permute-start.2) | collective-permute-done | bytes 262176 | tf_op jit(solution)/shard_map/ppermute | solution.py:50
  30.6 2.5 collective-permute-start.3
  33.1 0.7 bitcast_dynamic-update-slice_fusion.12
  33.8 7.1 %collective-permute-done.3 = bf16[2048,64]{0,1:T(8,128)(2,1)S(1)} collective-permute-done((bf16[2048,64]{0,1:T(8,128)(2,1)S(1)}, bf16[2048,64]{0,1:T(8,128)(2,1)S(1)}, u32[]{:S(2)}, u32[]{:S(2)}) %collective-permute-start.3) | collective-permute-done | bytes 262176 | tf_op jit(solution)/shard_map/ppermute | solution.py:50
  40.9 0.7 bitcast_dynamic-update-slice_fusion.11
  41.6 13.4 %collective-permute-done.4 = bf16[2048,64]{0,1:T(8,128)(2,1)S(1)} collective-permute-done((bf16[2048,64]{0,1:T(8,128)(2,1)S(1)}, bf16[2048,64]{0,1:T(8,128)(2,1)S(1)}, u32[]{:S(2)}, u32[]{:S(2)}) %collective-permute-start.4) | collective-permute-done | bytes 262176 | tf_op jit(solution)/shard_map/ppermute | solution.py:50
  55.0 0.7 bitcast_dynamic-update-slice_fusion.10
  55.7 13.1 %collective-permute-done.5 = bf16[2048,64]{0,1:T(8,128)(2,1)S(1)} collective-permute-done((bf16[2048,64]{0,1:T(8,128)(2,1)S(1)}, bf16[2048,64]{0,1:T(8,128)(2,1)S(1)}, u32[]{:S(2)}, u32[]{:S(2)}) %collective-permute-start.5) | collective-permute-done | bytes 262176 | tf_op jit(solution)/shard_map/ppermute | solution.py:50
  68.8 0.7 bitcast_dynamic-update-slice_fusion.9
  69.6 8.1 %collective-permute-done.6 = bf16[2048,64]{0,1:T(8,128)(2,1)S(1)} collective-permute-done((bf16[2048,64]{0,1:T(8,128)(2,1)S(1)}, bf16[2048,64]{0,1:T(8,128)(2,1)S(1)}, u32[]{:S(2)}, u32[]{:S(2)}) %collective-permute-start.6) | collective-permute-done | bytes 262176 | tf_op jit(solution)/shard_map/ppermute | solution.py:50
  77.7 0.7 bitcast_dynamic-update-slice_fusion.8
  78.4 13.1 %collective-permute-done.7 = bf16[2048,64]{0,1:T(8,128)(2,1)S(1)} collective-permute-done((bf16[2048,64]{0,1:T(8,128)(2,1)S(1)}, bf16[2048,64]{0,1:T(8,128)(2,1)S(1)}, u32[]{:S(2)}, u32[]{:S(2)}) %collective-permute-start.7) | collective-permute-done | bytes 262176 | tf_op jit(solution)/shard_map/ppermute | solution.py:50
  91.5 0.7 bitcast_dynamic-update-slice_fusion.7
  92.2 13.4 %collective-permute-done.8 = bf16[2048,64]{0,1:T(8,128)(2,1)S(1)} collective-permute-done((bf16[2048,64]{0,1:T(8,128)(2,1)S(1)}, bf16[2048,64]{0,1:T(8,128)(2,1)S(1)}, u32[]{:S(2)}, u32[]{:S(2)}) %collective-permute-start.8) | collective-permute-done | bytes 262176 | tf_op jit(solution)/shard_map/ppermute | solution.py:50
  105.6 0.7 bitcast_dynamic-update-slice_fusion.6
  106.3 13.5 %collective-permute-done.9 = bf16[2048,64]{0,1:T(8,128)(2,1)S(1)} collective-permute-done((bf16[2048,64]{0,1:T(8,128)(2,1)S(1)}, bf16[2048,64]{0,1:T(8,128)(2,1)S(1)}, u32[]{:S(2)}, u32[]{:S(2)}) %collective-permute-start.9) | collective-permute-done | bytes 262176 | tf_op jit(solution)/shard_map/ppermute | solution.py:50
  119.8 0.7 bitcast_dynamic-update-slice_fusion.5
  120.5 13.4 %collective-permute-done.10 = bf16[2048,64]{0,1:T(8,128)(2,1)S(1)} collective-permute-done((bf16[2048,64]{0,1:T(8,128)(2,1)S(1)}, bf16[2048,64]{0,1:T(8,128)(2,1)S(1)}, u32[]{:S(2)}, u32[]{:S(2)}) %collective-permute-start.10) | collective-permute-done | bytes 262176 | tf_op jit(solution)/shard_map/ppermute | solution.py:50
  133.9 0.7 bitcast_dynamic-update-slice_fusion.4
  134.6 13.1 %collective-permute-done.11 = bf16[2048,64]{0,1:T(8,128)(2,1)S(1)} collective-permute-done((bf16[2048,64]{0,1:T(8,128)(2,1)S(1)}, bf16[2048,64]{0,1:T(8,128)(2,1)S(1)}, u32[]{:S(2)}, u32[]{:S(2)}) %collective-permute-start.11) | collective-permute-done | bytes 262176 | tf_op jit(solution)/shard_map/ppermute | solution.py:50
  147.7 0.7 bitcast_dynamic-update-slice_fusion.3
  148.4 13.7 %collective-permute-done.12 = bf16[2048,64]{0,1:T(8,128)(2,1)S(1)} collective-permute-done((bf16[2048,64]{0,1:T(8,128)(2,1)S(1)}, bf16[2048,64]{0,1:T(8,128)(2,1)S(1)}, u32[]{:S(2)}, u32[]{:S(2)}) %collective-permute-start.12) | collective-permute-done | bytes 262176 | tf_op jit(solution)/shard_map/ppermute | solution.py:50
  162.2 0.7 bitcast_dynamic-update-slice_fusion.2
  162.9 7.4 %collective-permute-done.13 = bf16[2048,64]{0,1:T(8,128)(2,1)S(1)} collective-permute-done((bf16[2048,64]{0,1:T(8,128)(2,1)S(1)}, bf16[2048,64]{0,1:T(8,128)(2,1)S(1)}, u32[]{:S(2)}, u32[]{:S(2)}) %collective-permute-start.13) | collective-permute-done | bytes 262176 | tf_op jit(solution)/shard_map/ppermute | solution.py:50
  170.3 0.7 bitcast_dynamic-update-slice_fusion.1
  171.0 7.8 %collective-permute-done.14 = bf16[2048,64]{0,1:T(8,128)(2,1)S(1)} collective-permute-done((bf16[2048,64]{0,1:T(8,128)(2,1)S(1)}, bf16[2048,64]{0,1:T(8,128)(2,1)S(1)}, u32[]{:S(2)}, u32[]{:S(2)}) %collective-permute-start.14) | collective-permute-done | bytes 262176 | tf_op jit(solution)/shard_map/ppermute | solution.py:50
  178.8 0.7 bitcast_dynamic-update-slice_fusion
  179.5 5.1 %gather_fusion = bf16[16,2048,64]{1,2,0:T(8,128)(2,1)} fusion(bf16[16,2048,64]{1,2,0:T(8,128)(2,1)} %bitcast_dynamic-update-slice_fusion, s32[1024]{0:T(1024)S(1)} %pad_clamp_fusion), kind=kCustom, calls=%fused_computation | custom fusion | bytes 8388672 | tf_op jit(solution)/shard_map/gather | solution.py:52
  184.6 8.2 %fusion.18 = bf16[128,2048]{1,0:T(8,128)(2,1)S(1)} fusion(bf16[128,4096]{1,0:T(8,128)(2,1)S(1)} %copy-done.1, bf16[4096,2048]{1,0:T(8,128)(2,1)} %all-gather.3.cloned.1.call-done, bf16[128]{0:T(256)(128)(2,1)S(1)} %fusion.38), kind=kOutput, calls=%fused_computation.32 | convolution fusion | flops 2148007936 | bytes 18350336 | tf_op jit(solution)/shard_map/dot_general | solution.py:58
  192.7 9.9 %fusion.37 = f32[1024,2048]{1,0:T(8,128)} fusion(bf16[128,2048]{1,0:T(8,128)(2,1)S(1)} %fusion.18, bf16[2048,1024]{0,1:T(8,128)(2,1)} %bitcast.54, bf16[128,2048]{1,0:T(8,128)(2,1)} %param.10), kind=kOutput, calls=%fused_computation.40 | convolution fusion | flops 1073872896 | bytes 13631488 | tf_op jit(solution)/shard_map/dot_general | solution.py:70
  202.6 194.6 %all-reduce.2 = (bf16[1024,2048]{1,0:T(8,128)(2,1)}, f32[]{:T(128)}) all-reduce(f32[1024,2048]{1,0:T(8,128)} %fusion.37, f32[]{:T(128)} %convert_reduce_fusion), channel_id=1, replica_groups=mesh['groups'=2,'wide'=16] {'wide'}, use_global_device_ids=true, to_apply=%region_0.1 | all-reduce | flops 2097153 | bytes 12582920 | tf_op jit(solution)/shard_map/psum | solution.py:73
  398.6 6.9 %fusion.19 = f32[384]{0:T(512)S(1)} fusion(bf16[1024,384]{1,0:T(8,128)(2,1)S(1)} %copy-done.4, bf16[2048,384]{1,0:T(8,128)(2,1)S(1)} %copy-done, bf16[1024,2048]{1,0:T(8,128)(2,1)} %get-tuple-element.5, bf16[1024,2048]{1,0:T(8,128)(2,1)} %all-gather.5.cloned.1.call-done, f32[]{:T(128)} %bitcast.19), kind=kOutput, calls=%fused_computation.33 | convolution fusion | flops 1622277760 | bytes 10749444 | tf_op jit(solution)/shard_map/dot_general | solution.py:27
  405.5 3.0 fusion.20
  408.5 2.9 fusion.21
  411.4 3.0 fusion.22
  414.5 3.3 fusion.23
  417.7 2.9 fusion.24
  (41 shorter events, 1.5 us)
Async XLA Ops:
  6.5 392.0 %copy-start = (bf16[2048,384]{1,0:T(8,128)(2,1)S(1)}, bf16[2048,384]{1,0:T(8,128)(2,1)}, u32[]{:S(2)}) copy-start(bf16[2048,384]{1,0:T(8,128)(2,1)} %param.18) | copy-start | bytes 4718596
  6.5 178.0 %all-gather.3.cloned.1.call-start = ((), (), s32[]{:S(2)}) async-start(), calls=%async_computation | async-start | bytes 17825792 | tf_op jit(solution)/shard_map/all_gather | solution.py:60
  7.3 391.3 %all-gather.5.cloned.1.call-start = ((), (), s32[]{:S(2)}) async-start(), calls=%async_computation.1 | async-start | bytes 4456448 | tf_op jit(solution)/shard_map/all_gather | solution.py:76
  7.3 7.5 %collective-permute-start = (bf16[2048,64]{0,1:T(8,128)(2,1)}, bf16[2048,64]{0,1:T(8,128)(2,1)S(1)}, u32[]{:S(2)}, u32[]{:S(2)}) collective-permute-start(bf16[2048,64]{0,1:T(8,128)(2,1)} %param.13), channel_id=1, source_target_pairs={{0,1},{1,2},{2,3},{3,4},{4,5},{5,6},{6,7},{7,8},{8,9},{9,10},{10,1... | collective-permute-start | bytes 786440 | tf_op jit(solution)/shard_map/ppermute | solution.py:50
  14.8 4.5 %collective-permute-start.1 = (bf16[2048,64]{0,1:T(8,128)(2,1)S(1)}, bf16[2048,64]{0,1:T(8,128)(2,1)S(1)}, u32[]{:S(2)}, u32[]{:S(2)}) collective-permute-start(bf16[2048,64]{0,1:T(8,128)(2,1)S(1)} %collective-permute-done), channel_id=1, source_target_pairs={{0,1},{1,2},{2,3},{3,4},{4,5},{5,6},{6,7},{7,8},{8,9},{9,10},{10,1... | collective-permute-start | bytes 786440 | tf_op jit(solution)/shard_map/ppermute | solution.py:50
  19.3 11.3 %collective-permute-start.2 = (bf16[2048,64]{0,1:T(8,128)(2,1)S(1)}, bf16[2048,64]{0,1:T(8,128)(2,1)S(1)}, u32[]{:S(2)}, u32[]{:S(2)}) collective-permute-start(bf16[2048,64]{0,1:T(8,128)(2,1)S(1)} %collective-permute-done.1), channel_id=1, source_target_pairs={{0,1},{1,2},{2,3},{3,4},{4,5},{5,6},{6,7},{7,8},{8,9},{9,10},{10,1... | collective-permute-start | bytes 786440 | tf_op jit(solution)/shard_map/ppermute | solution.py:50
  30.6 10.3 %collective-permute-start.3 = (bf16[2048,64]{0,1:T(8,128)(2,1)S(1)}, bf16[2048,64]{0,1:T(8,128)(2,1)S(1)}, u32[]{:S(2)}, u32[]{:S(2)}) collective-permute-start(bf16[2048,64]{0,1:T(8,128)(2,1)S(1)} %collective-permute-done.2), channel_id=1, source_target_pairs={{0,1},{1,2},{2,3},{3,4},{4,5},{5,6},{6,7},{7,8},{8,9},{9,10},{10,1... | collective-permute-start | bytes 786440 | tf_op jit(solution)/shard_map/ppermute | solution.py:50
  40.9 14.1 %collective-permute-start.4 = (bf16[2048,64]{0,1:T(8,128)(2,1)S(1)}, bf16[2048,64]{0,1:T(8,128)(2,1)S(1)}, u32[]{:S(2)}, u32[]{:S(2)}) collective-permute-start(bf16[2048,64]{0,1:T(8,128)(2,1)S(1)} %collective-permute-done.3), channel_id=1, source_target_pairs={{0,1},{1,2},{2,3},{3,4},{4,5},{5,6},{6,7},{7,8},{8,9},{9,10},{10,1... | collective-permute-start | bytes 786440 | tf_op jit(solution)/shard_map/ppermute | solution.py:50
  55.0 13.8 %collective-permute-start.5 = (bf16[2048,64]{0,1:T(8,128)(2,1)S(1)}, bf16[2048,64]{0,1:T(8,128)(2,1)S(1)}, u32[]{:S(2)}, u32[]{:S(2)}) collective-permute-start(bf16[2048,64]{0,1:T(8,128)(2,1)S(1)} %collective-permute-done.4), channel_id=1, source_target_pairs={{0,1},{1,2},{2,3},{3,4},{4,5},{5,6},{6,7},{7,8},{8,9},{9,10},{10,1... | collective-permute-start | bytes 786440 | tf_op jit(solution)/shard_map/ppermute | solution.py:50
  68.8 8.9 %collective-permute-start.6 = (bf16[2048,64]{0,1:T(8,128)(2,1)S(1)}, bf16[2048,64]{0,1:T(8,128)(2,1)S(1)}, u32[]{:S(2)}, u32[]{:S(2)}) collective-permute-start(bf16[2048,64]{0,1:T(8,128)(2,1)S(1)} %collective-permute-done.5), channel_id=1, source_target_pairs={{0,1},{1,2},{2,3},{3,4},{4,5},{5,6},{6,7},{7,8},{8,9},{9,10},{10,1... | collective-permute-start | bytes 786440 | tf_op jit(solution)/shard_map/ppermute | solution.py:50
  77.7 13.8 %collective-permute-start.7 = (bf16[2048,64]{0,1:T(8,128)(2,1)S(1)}, bf16[2048,64]{0,1:T(8,128)(2,1)S(1)}, u32[]{:S(2)}, u32[]{:S(2)}) collective-permute-start(bf16[2048,64]{0,1:T(8,128)(2,1)S(1)} %collective-permute-done.6), channel_id=1, source_target_pairs={{0,1},{1,2},{2,3},{3,4},{4,5},{5,6},{6,7},{7,8},{8,9},{9,10},{10,1... | collective-permute-start | bytes 786440 | tf_op jit(solution)/shard_map/ppermute | solution.py:50
  91.5 14.1 %collective-permute-start.8 = (bf16[2048,64]{0,1:T(8,128)(2,1)S(1)}, bf16[2048,64]{0,1:T(8,128)(2,1)S(1)}, u32[]{:S(2)}, u32[]{:S(2)}) collective-permute-start(bf16[2048,64]{0,1:T(8,128)(2,1)S(1)} %collective-permute-done.7), channel_id=1, source_target_pairs={{0,1},{1,2},{2,3},{3,4},{4,5},{5,6},{6,7},{7,8},{8,9},{9,10},{10,1... | collective-permute-start | bytes 786440 | tf_op jit(solution)/shard_map/ppermute | solution.py:50
  105.6 14.2 %collective-permute-start.9 = (bf16[2048,64]{0,1:T(8,128)(2,1)S(1)}, bf16[2048,64]{0,1:T(8,128)(2,1)S(1)}, u32[]{:S(2)}, u32[]{:S(2)}) collective-permute-start(bf16[2048,64]{0,1:T(8,128)(2,1)S(1)} %collective-permute-done.8), channel_id=1, source_target_pairs={{0,1},{1,2},{2,3},{3,4},{4,5},{5,6},{6,7},{7,8},{8,9},{9,10},{10,1... | collective-permute-start | bytes 786440 | tf_op jit(solution)/shard_map/ppermute | solution.py:50
  119.8 14.1 %collective-permute-start.10 = (bf16[2048,64]{0,1:T(8,128)(2,1)S(1)}, bf16[2048,64]{0,1:T(8,128)(2,1)S(1)}, u32[]{:S(2)}, u32[]{:S(2)}) collective-permute-start(bf16[2048,64]{0,1:T(8,128)(2,1)S(1)} %collective-permute-done.9), channel_id=1, source_target_pairs={{0,1},{1,2},{2,3},{3,4},{4,5},{5,6},{6,7},{7,8},{8,9},{9,10},{10,1... | collective-permute-start | bytes 786440 | tf_op jit(solution)/shard_map/ppermute | solution.py:50
  133.9 13.8 %collective-permute-start.11 = (bf16[2048,64]{0,1:T(8,128)(2,1)S(1)}, bf16[2048,64]{0,1:T(8,128)(2,1)S(1)}, u32[]{:S(2)}, u32[]{:S(2)}) collective-permute-start(bf16[2048,64]{0,1:T(8,128)(2,1)S(1)} %collective-permute-done.10), channel_id=1, source_target_pairs={{0,1},{1,2},{2,3},{3,4},{4,5},{5,6},{6,7},{7,8},{8,9},{9,10},{10,1... | collective-permute-start | bytes 786440 | tf_op jit(solution)/shard_map/ppermute | solution.py:50
  147.7 14.5 %collective-permute-start.12 = (bf16[2048,64]{0,1:T(8,128)(2,1)S(1)}, bf16[2048,64]{0,1:T(8,128)(2,1)S(1)}, u32[]{:S(2)}, u32[]{:S(2)}) collective-permute-start(bf16[2048,64]{0,1:T(8,128)(2,1)S(1)} %collective-permute-done.11), channel_id=1, source_target_pairs={{0,1},{1,2},{2,3},{3,4},{4,5},{5,6},{6,7},{7,8},{8,9},{9,10},{10,1... | collective-permute-start | bytes 786440 | tf_op jit(solution)/shard_map/ppermute | solution.py:50
  162.2 8.1 %collective-permute-start.13 = (bf16[2048,64]{0,1:T(8,128)(2,1)S(1)}, bf16[2048,64]{0,1:T(8,128)(2,1)S(1)}, u32[]{:S(2)}, u32[]{:S(2)}) collective-permute-start(bf16[2048,64]{0,1:T(8,128)(2,1)S(1)} %collective-permute-done.12), channel_id=1, source_target_pairs={{0,1},{1,2},{2,3},{3,4},{4,5},{5,6},{6,7},{7,8},{8,9},{9,10},{10,1... | collective-permute-start | bytes 786440 | tf_op jit(solution)/shard_map/ppermute | solution.py:50
  170.3 8.5 %collective-permute-start.14 = (bf16[2048,64]{0,1:T(8,128)(2,1)S(1)}, bf16[2048,64]{0,1:T(8,128)(2,1)S(1)}, u32[]{:S(2)}, u32[]{:S(2)}) collective-permute-start(bf16[2048,64]{0,1:T(8,128)(2,1)S(1)} %collective-permute-done.13), channel_id=1, source_target_pairs={{0,1},{1,2},{2,3},{3,4},{4,5},{5,6},{6,7},{7,8},{8,9},{9,10},{10,1... | collective-permute-start | bytes 786440 | tf_op jit(solution)/shard_map/ppermute | solution.py:50
  179.5 5.1 %copy-start.1 = (bf16[128,4096]{1,0:T(8,128)(2,1)S(1)}, bf16[128,4096]{1,0:T(8,128)(2,1)}, u32[]{:S(2)}) copy-start(bf16[128,4096]{1,0:T(8,128)(2,1)} %param.11) | copy-start | bytes 3145732
  202.6 195.3 %copy-start.5 = (s32[6]{0:T(128)S(1)}, s32[6]{0:T(128)}, u32[]{:S(2)}) copy-start(s32[6]{0:T(128)} %param.16) | copy-start | bytes 76
  202.6 196.0 %copy-start.4 = (bf16[1024,384]{1,0:T(8,128)(2,1)S(1)}, bf16[1024,384]{1,0:T(8,128)(2,1)}, u32[]{:S(2)}) copy-start(bf16[1024,384]{1,0:T(8,128)(2,1)} %param.17) | copy-start | bytes 2359300
  398.6 6.9 %copy-start.2 = (bf16[1024,2048]{1,0:T(8,128)(2,1)S(1)}, bf16[1024,2048]{1,0:T(8,128)(2,1)}, u32[]{:S(2)}) copy-start(bf16[1024,2048]{1,0:T(8,128)(2,1)} %all-gather.5.cloned.1.call-done) | copy-start | bytes 12582916
  398.6 6.9 %copy-start.3 = (bf16[1024,2048]{1,0:T(8,128)(2,1)S(1)}, bf16[1024,2048]{1,0:T(8,128)(2,1)}, u32[]{:S(2)}) copy-start(bf16[1024,2048]{1,0:T(8,128)(2,1)} %get-tuple-element.5) | copy-start | bytes 12582916
Sparse Core Ops, SparseCore 0:
  9.5 154.9 all-gather.2
  166.7 59.6 all-gather.4
